TPU v7x, 32 devices: a whole 2x2x4 slice. The times are simulated.
32 devices in a mesh: clips: 2 (over y), rows: 4 (over z), tm: 2 (over x), chan: 2 (over core).
Axes of the slice: x: 2, y: 2, z: 4, core: 2. Of those that a mesh axis runs over, the one named last changes fastest.
Arguments:
- latent: bfloat16 [8, 4, 64, 512], P(('clips', 'tm'), 'rows', None, 'chan'), parts along dimension 0, may hold values from -24 to 24, as said below
- norm1_gain: float32 [512], P('chan'), may hold values from 0.5 to 1.5
- norm1_bias: float32 [512], P('chan'), may hold values from -1.2 to 1.2
- conv_weight: bfloat16 [13824, 512], P('rows', 'chan'), may hold values from -0.0546875 to 0.0546875
- conv_bias: float32 [512], P('chan'), may hold values from -1.2 to 1.2
- norm2_gain: float32 [512], P('chan'), may hold values from 0.5 to 1.5
- norm2_bias: float32 [512], P('chan'), may hold values from -1.2 to 1.2
- w_query: bfloat16 [512, 512], replicated, may hold values from -2 to 2
- b_query: float32 [512], replicated, may hold values from -1.2 to 1.2
- w_key: bfloat16 [512, 512], replicated, may hold values from -3 to 3
- w_value: bfloat16 [512, 512], replicated, may hold values from -0.25 to 0.25
- b_value: float32 [512], replicated, may hold values from -1.2 to 1.2
- w_out: bfloat16 [512, 512], replicated, may hold values from -0.25 to 0.25
- b_out: float32 [512], replicated, may hold values from -1.2 to 1.2
Outputs:
- decoded: bfloat16 [8, 4, 64, 512], P(('clips', 'tm'), 'rows', None, 'chan'), parts along dimension 0
There are 2 independent parts, one for each index of `clips`. A program takes and returns all parts, laid end to end along the dimension named above; an argument that names none is the same for every part. Nothing has to cross between parts.
Inputs may be any that keep to these rules, and one draw needn't show every extreme that they name: `latent`: activations of order one.
All inputs are finite; a program needn't handle non-finite values.
Results may differ from a plain program's by a relative error of at most 0.012.
The roundings to bfloat16 on the way count: a program that leaves them out, or rounds other values in their place, can miss the bound.
Values may be sent and summed in bfloat16 or wider, within the bound.
No kernel may reach another device: no remote copies, remote signals or barrier semaphores. Data moves between devices by JAX's collectives and lax.ppermute only.
A program may use at most 64 MiB of HBM per device.

v0:
```python
import jax
import jax.numpy as jnp
from jax import lax
from jax.sharding import PartitionSpec as P

C = 512
GROUPS = 32
EPSILON = 1e-06


def passed_along(value, axis, steps):
    count = lax.axis_size(axis)
    leading, last = (max(0, -steps), min(count, count - steps))
    return lax.ppermute(value, axis, [(source, source + steps) for source in range(leading, last)])


def with_halo(cells, sides, width):
    for axis, dim in sides:
        count = lax.axis_size(axis)
        ends = count - 1
        head = lax.slice_in_dim(cells, 0, width, axis=dim)
        tail = lax.slice_in_dim(cells, cells.shape[dim] - width, cells.shape[dim], axis=dim)
        cells = jnp.concatenate(
            [
                lax.ppermute(tail, axis, [(i, (i + 1) % count) for i in range(ends)]),
                cells,
                lax.ppermute(head, axis, [((i + 1) % count, i) for i in range(ends)]),
            ],
            axis=dim,
        )
    return cells


def group_view(values, group_size):
    full_shape = values.shape
    return values.astype(jnp.float32).reshape(
        full_shape[:-1] + (full_shape[-1] // group_size, group_size)
    )


def clip_normalize(latent, group_size):
    grouped = group_view(latent, group_size)
    cell_count = (
        grouped.shape[0]
        * grouped.shape[1]
        * grouped.shape[2]
        * group_size
        * lax.axis_size("rows")
        * lax.axis_size("tm")
    )
    group_mean = lax.psum(jnp.sum(grouped, axis=(0, 1, 2, 4)), ("rows", "tm")) / cell_count
    centered = grouped - group_mean[:, None]
    group_var = (
        lax.psum(jnp.sum(centered * centered, axis=(0, 1, 2, 4)), ("rows", "tm")) / cell_count
    )
    centered = grouped - group_mean[:, None]
    return (centered * lax.rsqrt(group_var + EPSILON)[:, None]).reshape(latent.shape)


def frame_normalize(middle, group_size):
    grouped = group_view(middle, group_size)
    cell_count = grouped.shape[1] * grouped.shape[2] * group_size * lax.axis_size("rows")
    group_mean = lax.psum(jnp.sum(grouped, axis=(1, 2, 4)), "rows") / cell_count
    centered = grouped - group_mean[:, None, None, :, None]
    group_var = lax.psum(jnp.sum(centered * centered, axis=(1, 2, 4)), "rows") / cell_count
    centered = grouped - group_mean[:, None, None, :, None]
    return (centered * lax.rsqrt(group_var + EPSILON)[:, None, None, :, None]).reshape(middle.shape)


def softmax_update(running, queries, key_block, value_block, score_scale):
    row_peak, weight_sum, accumulated = running
    scores = (
        jnp.einsum("fqc,fkc->fqk", queries, key_block, preferred_element_type=jnp.float32)
        * score_scale
    )
    new_peak = jnp.max(scores, axis=2)
    factor = jnp.exp(row_peak - new_peak)
    weights = jnp.exp(scores - new_peak[:, :, None])
    weight_sum = weight_sum * factor + jnp.sum(weights, axis=2)
    accumulated = accumulated * factor[:, :, None] + jnp.einsum(
        "fqk,fkc->fqc",
        weights.astype(jnp.bfloat16),
        value_block,
        preferred_element_type=jnp.float32,
    )
    return (new_peak, weight_sum, accumulated)


def local(
    latent,
    norm1_gain,
    norm1_bias,
    conv_weight,
    conv_bias,
    norm2_gain,
    norm2_bias,
    w_query,
    b_query,
    w_key,
    w_value,
    b_value,
    w_out,
    b_out,
):
    frames, rows_here, columns, channels = latent.shape
    group_size = C // GROUPS
    activated = jax.nn.silu(clip_normalize(latent, group_size) * norm1_gain + norm1_bias).astype(
        jnp.bfloat16
    )
    all_channels = lax.all_gather(activated, "chan", axis=3, tiled=True)
    carried = passed_along(all_channels, "tm", 1)
    carried = jnp.where(
        lax.axis_index("tm") == 0, jnp.broadcast_to(all_channels[:1], carried.shape), carried
    )
    timed = jnp.concatenate([carried, all_channels], axis=0)
    rimmed = with_halo(timed, (("rows", 1),), 1)
    row_place = lax.axis_index("rows")
    upper_rim = jnp.where(row_place == 0, rimmed[:, 1:2], rimmed[:, :1])
    lower_rim = jnp.where(row_place == lax.axis_size("rows") - 1, rimmed[:, -2:-1], rimmed[:, -1:])
    rimmed = jnp.concatenate([upper_rim, rimmed[:, 1:-1], lower_rim], axis=1)
    padded = jnp.concatenate([rimmed[:, :, :1], rimmed, rimmed[:, :, -1:]], axis=2)
    windows = []
    for frame_step in range(3):
        for row_step in range(3):
            for column_step in range(3):
                windows.append(
                    padded[
                        frame_step : frame_step + frames,
                        row_step : row_step + rows_here,
                        column_step : column_step + columns,
                    ].reshape(-1, C)
                )
    patches = jnp.concatenate(windows, axis=1)
    convolved = jnp.dot(
        patches,
        lax.all_gather(conv_weight, "rows", axis=0, tiled=True),
        preferred_element_type=jnp.float32,
    )
    middle = (latent.astype(jnp.float32) + (convolved + conv_bias).reshape(latent.shape)).astype(
        jnp.bfloat16
    )
    normed = (frame_normalize(middle, group_size) * norm2_gain + norm2_bias).astype(jnp.bfloat16)
    swapped = lax.all_to_all(normed, "chan", split_axis=0, concat_axis=3, tiled=True)
    frame_count = swapped.shape[0]
    local_tokens = rows_here * columns
    flattened = swapped.reshape(-1, C)
    queries = (
        (jnp.dot(flattened, w_query, preferred_element_type=jnp.float32) + b_query)
        .astype(jnp.bfloat16)
        .reshape(frame_count, local_tokens, C)
    )
    score_scale = C ** (-0.5)
    initial = (
        jnp.full((frame_count, local_tokens), -jnp.inf, jnp.float32),
        jnp.zeros((frame_count, local_tokens), jnp.float32),
        jnp.zeros((frame_count, local_tokens, C), jnp.float32),
    )
    feature_rows = swapped.reshape(frame_count, local_tokens, C)
    shard_flat = lax.all_gather(feature_rows, "rows", axis=1, tiled=True).reshape(-1, C)
    key_block = (
        jnp.dot(shard_flat, w_key, preferred_element_type=jnp.float32)
        .astype(jnp.bfloat16)
        .reshape(frame_count, -1, C)
    )
    value_block = (
        (jnp.dot(shard_flat, w_value, preferred_element_type=jnp.float32) + b_value)
        .astype(jnp.bfloat16)
        .reshape(frame_count, -1, C)
    )
    row_peak, weight_sum, accumulated = softmax_update(
        initial, queries, key_block, value_block, score_scale
    )
    attended = (accumulated / weight_sum[:, :, None]).astype(jnp.bfloat16)
    branch = (
        (jnp.dot(attended.reshape(-1, C), w_out, preferred_element_type=jnp.float32) + b_out)
        .astype(jnp.bfloat16)
        .reshape(frame_count, rows_here, columns, C)
    )
    returned = lax.all_to_all(branch, "chan", split_axis=3, concat_axis=0, tiled=True)
    return (middle.astype(jnp.float32) + returned.astype(jnp.float32)).astype(jnp.bfloat16)


def solution(mesh):
    in_specs = (
        P(("clips", "tm"), "rows", None, "chan"),
        P("chan"),
        P("chan"),
        P("rows", "chan"),
        P("chan"),
        P("chan"),
        P("chan"),
        P(),
        P(),
        P(),
        P(),
        P(),
        P(),
        P(),
    )
    out_specs = P(("clips", "tm"), "rows", None, "chan")
    return jax.shard_map(local, mesh=mesh, in_specs=in_specs, out_specs=out_specs, check_vma=False)
```

profile of v0, /device:TPU:0, one launch (start us, length us, event | category | flops | bytes accessed | tf_op | source)
XLA Modules:
  0.0 204.5 jit_solution(6646806189756094243)
XLA Ops:
  6.5 0.7 all-gather.2.cloned.1.call-update
  7.3 0.9 convert_reduce_fusion.1
  8.3 23.4 %psum.28 = f32[16]{0:T(128)S(1)} all-reduce(f32[16]{0:T(128)S(1)} %reduce_sum.59), channel_id=1, replica_groups=mesh['clips'=2,'rows'=4,'tm'=2,'chan'=2] {'rows','tm'}, use_global_device_ids=true, to_apply=%region_2.0 | all-reduce | flops 16 | bytes 128 | tf_op jit(solution)/shard_map/psum | solution.py:51
  31.9 0.9 fusion.39
  33.0 17.6 %psum.29 = f32[16]{0:T(128)S(1)} all-reduce(f32[16]{0:T(128)S(1)} %reduce_sum.62), channel_id=1, replica_groups=mesh['clips'=2,'rows'=4,'tm'=2,'chan'=2] {'rows','tm'}, use_global_device_ids=true, to_apply=%region_5.6 | all-reduce | flops 16 | bytes 128 | tf_op jit(solution)/shard_map/psum | solution.py:54
  50.8 0.9 fusion.47
  51.7 1.9 all_gather.9
  53.6 3.9 %collective-permute-start = (bf16[2,1,64,512]{3,2,1,0:T(8,128)(2,1)S(1)}, bf16[2,1,64,512]{3,2,1,0:T(8,128)(2,1)S(1)}, u32[]{:S(2)}, u32[]{:S(2)}) collective-permute-start(bf16[2,1,64,512]{3,2,1,0:T(8,128)(2,1)S(1)} %all_gather.9), channel_id=1, source_target_pairs={{0,2},{1,3},{4,6},{5,7},{8,10},{9,11},{12,14},{13,15},{16,18},{17,... | collective-permute-start | bytes 393224 | tf_op jit(solution)/shard_map/ppermute | solution.py:14
  57.5 3.0 %collective-permute-done = bf16[2,1,64,512]{3,2,1,0:T(8,128)(2,1)S(1)} collective-permute-done((bf16[2,1,64,512]{3,2,1,0:T(8,128)(2,1)S(1)}, bf16[2,1,64,512]{3,2,1,0:T(8,128)(2,1)S(1)}, u32[]{:S(2)}, u32[]{:S(2)}) %collective-permute-start) | collective-permute-done | bytes 131104 | tf_op jit(solution)/shard_map/ppermute | solution.py:14
  60.6 2.1 %collective-permute-start.1 = (bf16[4,1,64,512]{3,2,1,0:T(8,128)(2,1)S(1)}, bf16[4,1,64,512]{3,2,1,0:T(8,128)(2,1)S(1)}, u32[]{:S(2)}, u32[]{:S(2)}) collective-permute-start(bf16[4,1,64,512]{3,2,1,0:T(8,128)(2,1)S(1)} %pad_maximum_fusion.6), channel_id=1, source_target_pairs={{0,4},{4,8},{8,12},{1,5},{5,9},{9,13},{2,6},{6,10},{10,14},{3,7},{... | collective-permute-start | bytes 786440 | tf_op jit(solution)/shard_map/ppermute | solution.py:25
  62.7 1.3 collective-permute-start.2
  64.1 10.4 %collective-permute-done.1 = bf16[4,1,64,512]{3,2,1,0:T(8,128)(2,1)S(1)} collective-permute-done((bf16[4,1,64,512]{3,2,1,0:T(8,128)(2,1)S(1)}, bf16[4,1,64,512]{3,2,1,0:T(8,128)(2,1)S(1)}, u32[]{:S(2)}, u32[]{:S(2)}) %collective-permute-start.1) | collective-permute-done | bytes 262176 | tf_op jit(solution)/shard_map/ppermute | solution.py:25
  74.4 9.7 %collective-permute-done.2 = bf16[4,1,64,512]{3,2,1,0:T(8,128)(2,1)S(1)} collective-permute-done((bf16[4,1,64,512]{3,2,1,0:T(8,128)(2,1)S(1)}, bf16[4,1,64,512]{3,2,1,0:T(8,128)(2,1)S(1)}, u32[]{:S(2)}, u32[]{:S(2)}) %collective-permute-start.2) | collective-permute-done | bytes 262176 | tf_op jit(solution)/shard_map/ppermute | solution.py:27
  85.0 0.7 constant_dynamic-update-slice_fusion.26
  96.0 0.7 constant_dynamic-update-slice_fusion.10
  98.8 0.7 constant_dynamic-update-slice_fusion.6
  103.6 42.1 %all-gather.2.cloned.1.call-done = bf16[13824,256]{1,0:T(8,128)(2,1)} async-done(((bf16[3456,256]{1,0:T(8,128)(2,1)}), bf16[13824,256]{1,0:T(8,128)(2,1)}) %all-gather.2.cloned.1.call-update) | async-done | bytes 7077904 | tf_op jit(solution)/shard_map/all_gather | solution.py:136
  145.7 5.2 %convert_reduce_fusion = (f32[2,256]{1,0:T(2,128)S(1)}, bf16[2,1,64,256]{3,2,1,0:T(8,128)(2,1)S(1)}) fusion(bf16[2,1,64,256]{3,2,1,0:T(8,128)(2,1)S(1)} %copy-done.1, f32[256]{0:T(256)S(1)} %copy-done.5, bf16[13824,256]{1,0:T(8,128)(2,1)} %all-gather.2.cloned.1.call-done, bf16[128,13824]{1,0:T(8,128)(2,1)} %constant_dynamic-update-slice_fusion), kind=kOutput, calls=%fused_computation.49 | convolution fusion | flops 906165760 | bytes 10750976 | tf_op jit(solution)/shard_map/dot_general | solution.py:134
  151.1 8.7 %psum.30 = f32[2,16]{1,0:T(2,128)S(1)} all-reduce(f32[2,16]{1,0:T(2,128)S(1)} %reduce_sum.81), channel_id=1, replica_groups=mesh['clips'=2,'rows'=4,'tm'=2,'chan'=2] {'rows'}, use_global_device_ids=true, to_apply=%region_8.9 | all-reduce | flops 32 | bytes 256 | tf_op jit(solution)/shard_map/psum | solution.py:63
  160.1 10.1 %psum.31 = f32[2,16]{1,0:T(2,128)S(1)} all-reduce(f32[2,16]{1,0:T(2,128)S(1)} %reduce_sum.84), channel_id=1, replica_groups=mesh['clips'=2,'rows'=4,'tm'=2,'chan'=2] {'rows'}, use_global_device_ids=true, to_apply=%region_11.12 | all-reduce | flops 32 | bytes 256 | tf_op jit(solution)/shard_map/psum | solution.py:65
  170.4 3.8 %all_to_all.24 = bf16[2,1,64,256]{3,2,1,0:T(8,128)(2,1)S(1)} all-to-all(bf16[2,1,64,256]{3,2,1,0:T(8,128)(2,1)S(1)} %fusion.38), channel_id=1, replica_groups=mesh['clips'=2,'rows'=4,'tm'=2,'chan'=2] {'chan'}, dimensions={0} | all-to-all | bytes 131072 | tf_op jit(solution)/shard_map/all_to_all | solution.py:143
  174.3 14.3 %all_gather.11 = bf16[1,256,512]{2,1,0:T(8,128)(2,1)S(1)} all-gather(bf16[1,64,512]{2,1,0:T(8,128)(2,1)S(1)} %reshape.270), channel_id=1, replica_groups=mesh['clips'=2,'rows'=4,'tm'=2,'chan'=2] {'rows'}, dimensions={1}, use_global_device_ids=true | all-gather | bytes 327680 | tf_op jit(solution)/shard_map/all_gather | solution.py:159
  191.0 1.4 reduce.14
  192.6 3.8 %all_to_all.25 = bf16[2,2,8192]{2,1,0:T(2,128)(2,1)S(1)} all-to-all(bf16[2,2,8192]{2,1,0:T(2,128)(2,1)S(1)} %reshape.275), channel_id=1, replica_groups=mesh['clips'=2,'rows'=4,'tm'=2,'chan'=2] {'chan'}, dimensions={0} | all-to-all | bytes 131072 | tf_op jit(solution)/shard_map/all_to_all | solution.py:179
  (93 shorter events, 22.5 us)
Async XLA Ops:
  6.5 182.1 %copy-start = (bf16[512,512]{1,0:T(8,128)(2,1)S(1)}, bf16[512,512]{1,0:T(8,128)(2,1)}, u32[]{:S(2)}) copy-start(bf16[512,512]{1,0:T(8,128)(2,1)} %param.21) | copy-start | bytes 1572868
  6.5 139.1 %all-gather.2.cloned.1.call-start = ((), (), s32[]{:S(2)}) async-start(), calls=%async_computation.2 | async-start | bytes 8847360 | tf_op jit(solution)/shard_map/all_gather | solution.py:136
  53.6 6.9 %collective-permute-start = (bf16[2,1,64,512]{3,2,1,0:T(8,128)(2,1)S(1)}, bf16[2,1,64,512]{3,2,1,0:T(8,128)(2,1)S(1)}, u32[]{:S(2)}, u32[]{:S(2)}) collective-permute-start(bf16[2,1,64,512]{3,2,1,0:T(8,128)(2,1)S(1)} %all_gather.9), channel_id=1, source_target_pairs={{0,2},{1,3},{4,6},{5,7},{8,10},{9,11},{12,14},{13,15},{16,18},{17,... | collective-permute-start | bytes 393224 | tf_op jit(solution)/shard_map/ppermute | solution.py:14
  60.6 13.8 %collective-permute-start.1 = (bf16[4,1,64,512]{3,2,1,0:T(8,128)(2,1)S(1)}, bf16[4,1,64,512]{3,2,1,0:T(8,128)(2,1)S(1)}, u32[]{:S(2)}, u32[]{:S(2)}) collective-permute-start(bf16[4,1,64,512]{3,2,1,0:T(8,128)(2,1)S(1)} %pad_maximum_fusion.6), channel_id=1, source_target_pairs={{0,4},{4,8},{8,12},{1,5},{5,9},{9,13},{2,6},{6,10},{10,14},{3,7},{... | collective-permute-start | bytes 786440 | tf_op jit(solution)/shard_map/ppermute | solution.py:25
  62.7 21.4 %collective-permute-start.2 = (bf16[4,1,64,512]{3,2,1,0:T(8,128)(2,1)S(1)}, bf16[4,1,64,512]{3,2,1,0:T(8,128)(2,1)S(1)}, u32[]{:S(2)}, u32[]{:S(2)}) collective-permute-start(bf16[4,1,64,512]{3,2,1,0:T(8,128)(2,1)S(1)} %pad_maximum_fusion.6), channel_id=1, source_target_pairs={{4,0},{8,4},{12,8},{5,1},{9,5},{13,9},{6,2},{10,6},{14,10},{7,3},{... | collective-permute-start | bytes 786440 | tf_op jit(solution)/shard_map/ppermute | solution.py:27
  85.8 59.9 %copy-start.1 = (bf16[2,1,64,256]{3,2,1,0:T(8,128)(2,1)S(1)}, bf16[2,1,64,256]{3,2,1,0:T(8,128)(2,1)}, u32[]{:S(2)}) copy-start(bf16[2,1,64,256]{3,2,1,0:T(8,128)(2,1)} %param.14) | copy-start | bytes 196612
  85.8 59.9 %copy-start.5 = (f32[256]{0:T(256)S(1)}, f32[256]{0:T(256)}, u32[]{:S(2)}) copy-start(f32[256]{0:T(256)} %param.18) | copy-start | bytes 3076
  103.6 66.8 %copy-start.6 = (f32[256]{0:T(256)S(1)}, f32[256]{0:T(256)}, u32[]{:S(2)}) copy-start(f32[256]{0:T(256)} %param.20) | copy-start | bytes 3076
  103.6 66.8 %copy-start.7 = (f32[256]{0:T(256)S(1)}, f32[256]{0:T(256)}, u32[]{:S(2)}) copy-start(f32[256]{0:T(256)} %param.19) | copy-start | bytes 3076
  103.6 85.1 %copy-start.3 = (f32[512]{0:T(512)S(1)}, f32[512]{0:T(512)}, u32[]{:S(2)}) copy-start(f32[512]{0:T(512)} %param.22) | copy-start | bytes 6148
  103.6 85.3 %copy-start.8 = (bf16[512,512]{1,0:T(8,128)(2,1)S(1)}, bf16[512,512]{1,0:T(8,128)(2,1)}, u32[]{:S(2)}) copy-start(bf16[512,512]{1,0:T(8,128)(2,1)} %param.23) | copy-start | bytes 1572868
  103.6 86.1 %copy-start.9 = (bf16[512,512]{1,0:T(8,128)(2,1)S(1)}, bf16[512,512]{1,0:T(8,128)(2,1)}, u32[]{:S(2)}) copy-start(bf16[512,512]{1,0:T(8,128)(2,1)} %param.24) | copy-start | bytes 1572868
  103.6 86.1 %copy-start.10 = (f32[512]{0:T(512)S(1)}, f32[512]{0:T(512)}, u32[]{:S(2)}) copy-start(f32[512]{0:T(512)} %param.25) | copy-start | bytes 6148
  150.9 39.3 %copy-start.2 = (bf16[512,512]{1,0:T(8,128)(2,1)S(1)}, bf16[512,512]{1,0:T(8,128)(2,1)}, u32[]{:S(2)}) copy-start(bf16[512,512]{1,0:T(8,128)(2,1)} %param.26) | copy-start | bytes 1572868
  150.9 39.3 %copy-start.4 = (f32[512]{0:T(512)S(1)}, f32[512]{0:T(512)}, u32[]{:S(2)}) copy-start(f32[512]{0:T(512)} %param.27) | copy-start | bytes 6148
Sparse Core Ops, SparseCore 0:
  8.9 136.6 all-gather.1
where the time goes:
time: 205 us; the launch traced here: 204 us
  blocking collectives  83.6 us (41%)
  waiting for transfers between devices  65.9 us (32%)
  local copies, waits for them, and re-layouts  21.1 us (10%)
  between operations  13.7 us (7%)
  starting transfers between devices  7.29 us (4%)
  matrix products  6.57 us (3%)
  other arithmetic  6.28 us (3%)
    all_gather x1, waiting for transfers between devices, local(): lax.all_gather(conv_weight, 'rows', axis=0, tiled=True)  42.1 us
    psum x1, blocking collectives, clip_normalize(): lax.psum(jnp.sum(grouped, axis=(0, 1, 2, 4)), ('rows', 'tm')) / cell_count  23.4 us
    unnamed x52, local copies, waits for them, and re-layouts  18.7 us
    psum x1, blocking collectives, clip_normalize(): lax.psum(jnp.sum(centered * centered, axis=(0, 1, 2, 4)), ('rows', 'tm'))  17.6 us
    all_gather x1, blocking collectives, local(): lax.all_gather(feature_rows, 'rows', axis=1, tiled=True).reshape(-1, C)  14.3 us
    ppermute x1, waiting for transfers between devices, with_halo(): lax.ppermute(tail, axis, [(i, (i + 1) % count) for i in range(ends)])  10.4 us
    psum x1, blocking collectives, frame_normalize(): lax.psum(jnp.sum(centered * centered, axis=(1, 2, 4)), 'rows') / cell_count  10.1 us
    ppermute x1, waiting for transfers between devices, with_halo(): lax.ppermute(head, axis, [((i + 1) % count, i) for i in range(ends)])  9.72 us
  transfers between devices with their start and end apart: 4, of which 4 were waited for; matrix products, arithmetic and copies ran while one was open for 11% of the time, Pallas kernels for 0%

commit v1 on v0

--- a/solution.py
+++ b/solution.py
@@ -2,6 +2,7 @@
 import jax.numpy as jnp
 from jax import lax
 from jax.sharding import PartitionSpec as P
+from jax.lax import psum
 
 C = 512
 GROUPS = 32
@@ -51,7 +52,7 @@
     group_mean = lax.psum(jnp.sum(grouped, axis=(0, 1, 2, 4)), ("rows", "tm")) / cell_count
     centered = grouped - group_mean[:, None]
     group_var = (
-        lax.psum(jnp.sum(centered * centered, axis=(0, 1, 2, 4)), ("rows", "tm")) / cell_count
+        psum(psum(jnp.sum(centered * centered, axis=(0, 1, 2, 4)), "tm"), "rows") / cell_count
     )
     centered = grouped - group_mean[:, None]
     return (centered * lax.rsqrt(group_var + EPSILON)[:, None]).reshape(latent.shape)

time: 205 us -> 205 us (level)
  blocking collectives: 83.6 us -> 79.8 us
  waiting for transfers between devices: 65.9 us -> 68.8 us
    psum x1 -> x2, blocking collectives: 17.6 us -> 13.9 us  [the longest x1 8.94 us: clip_normalize(): psum(psum(jnp.sum(centered * centered, axis=(0, 1, 2, 4)), 'tm'), 'rows')]
where the time goes in v1:
time: 205 us; the launch traced here: 204 us
  blocking collectives  79.8 us (39%)
  waiting for transfers between devices  68.8 us (34%)
  local copies, waits for them, and re-layouts  21.1 us (10%)
  between operations  13.7 us (7%)
  starting transfers between devices  8.13 us (4%)
  matrix products  6.57 us (3%)
  other arithmetic  6.28 us (3%)
    all_gather x1, waiting for transfers between devices, local(): lax.all_gather(conv_weight, 'rows', axis=0, tiled=True)  43.8 us
    psum x1, blocking collectives, clip_normalize(): lax.psum(jnp.sum(grouped, axis=(0, 1, 2, 4)), ('rows', 'tm')) / cell_count  23.4 us
    unnamed x52, local copies, waits for them, and re-layouts  18.7 us
    all_gather x1, blocking collectives, local(): lax.all_gather(feature_rows, 'rows', axis=1, tiled=True).reshape(-1, C)  14.3 us
    ppermute x1, waiting for transfers between devices, with_halo(): lax.ppermute(head, axis, [((i + 1) % count, i) for i in range(ends)])  10.8 us
    ppermute x1, waiting for transfers between devices, with_halo(): lax.ppermute(tail, axis, [(i, (i + 1) % count) for i in range(ends)])  10.4 us
    psum x1, blocking collectives, frame_normalize(): lax.psum(jnp.sum(centered * centered, axis=(1, 2, 4)), 'rows') / cell_count  10 us
    psum x1, blocking collectives, clip_normalize(): psum(psum(jnp.sum(centered * centered, axis=(0, 1, 2, 4)), 'tm'), 'rows')  8.94 us
  transfers between devices with their start and end apart: 4, of which 4 were waited for; matrix products, arithmetic and copies ran while one was open for 11% of the time, Pallas kernels for 0%

profile of v1, /device:TPU:0, one launch (start us, length us, event | category | flops | bytes accessed | tf_op | source)
XLA Modules:
  0.0 204.4 jit_solution(12584682356806645970)
XLA Ops:
  6.5 0.7 all-gather.2.cloned.1.call-update
  7.3 0.9 convert_reduce_fusion.1
  8.3 23.4 %psum.35 = f32[16]{0:T(128)S(1)} all-reduce(f32[16]{0:T(128)S(1)} %reduce_sum.59), channel_id=1, replica_groups=mesh['clips'=2,'rows'=4,'tm'=2,'chan'=2] {'rows','tm'}, use_global_device_ids=true, to_apply=%region_2.0 | all-reduce | flops 16 | bytes 128 | tf_op jit(solution)/shard_map/psum | solution.py:52
  31.9 0.9 fusion.39
  33.0 4.9 %psum.36 = f32[16]{0:T(128)S(1)} all-reduce(f32[16]{0:T(128)S(1)} %reduce_sum.62), channel_id=1, replica_groups=mesh['clips'=2,'rows'=4,'tm'=2,'chan'=2] {'tm'}, use_global_device_ids=true, to_apply=%region_5.6 | all-reduce | flops 16 | bytes 128 | tf_op jit(solution)/shard_map/psum | solution.py:55
  37.9 8.9 %psum.37 = f32[16]{0:T(128)S(1)} all-reduce(f32[16]{0:T(128)S(1)} %psum.36), channel_id=1, replica_groups=mesh['clips'=2,'rows'=4,'tm'=2,'chan'=2] {'rows'}, use_global_device_ids=true, to_apply=%region_6.7 | all-reduce | flops 16 | bytes 128 | tf_op jit(solution)/shard_map/psum | solution.py:55
  47.0 0.9 fusion.47
  48.0 1.9 all_gather.9
  49.9 3.4 %collective-permute-start = (bf16[2,1,64,512]{3,2,1,0:T(8,128)(2,1)S(1)}, bf16[2,1,64,512]{3,2,1,0:T(8,128)(2,1)S(1)}, u32[]{:S(2)}, u32[]{:S(2)}) collective-permute-start(bf16[2,1,64,512]{3,2,1,0:T(8,128)(2,1)S(1)} %all_gather.9), channel_id=1, source_target_pairs={{0,2},{1,3},{4,6},{5,7},{8,10},{9,11},{12,14},{13,15},{16,18},{17,... | collective-permute-start | bytes 393224 | tf_op jit(solution)/shard_map/ppermute | solution.py:15
  53.3 3.0 %collective-permute-done = bf16[2,1,64,512]{3,2,1,0:T(8,128)(2,1)S(1)} collective-permute-done((bf16[2,1,64,512]{3,2,1,0:T(8,128)(2,1)S(1)}, bf16[2,1,64,512]{3,2,1,0:T(8,128)(2,1)S(1)}, u32[]{:S(2)}, u32[]{:S(2)}) %collective-permute-start) | collective-permute-done | bytes 131104 | tf_op jit(solution)/shard_map/ppermute | solution.py:15
  56.4 3.4 %collective-permute-start.1 = (bf16[4,1,64,512]{3,2,1,0:T(8,128)(2,1)S(1)}, bf16[4,1,64,512]{3,2,1,0:T(8,128)(2,1)S(1)}, u32[]{:S(2)}, u32[]{:S(2)}) collective-permute-start(bf16[4,1,64,512]{3,2,1,0:T(8,128)(2,1)S(1)} %pad_maximum_fusion.6), channel_id=1, source_target_pairs={{0,4},{4,8},{8,12},{1,5},{5,9},{9,13},{2,6},{6,10},{10,14},{3,7},{... | collective-permute-start | bytes 786440 | tf_op jit(solution)/shard_map/ppermute | solution.py:26
  59.8 1.3 collective-permute-start.2
  61.1 10.4 %collective-permute-done.1 = bf16[4,1,64,512]{3,2,1,0:T(8,128)(2,1)S(1)} collective-permute-done((bf16[4,1,64,512]{3,2,1,0:T(8,128)(2,1)S(1)}, bf16[4,1,64,512]{3,2,1,0:T(8,128)(2,1)S(1)}, u32[]{:S(2)}, u32[]{:S(2)}) %collective-permute-start.1) | collective-permute-done | bytes 262176 | tf_op jit(solution)/shard_map/ppermute | solution.py:26
  71.5 10.8 %collective-permute-done.2 = bf16[4,1,64,512]{3,2,1,0:T(8,128)(2,1)S(1)} collective-permute-done((bf16[4,1,64,512]{3,2,1,0:T(8,128)(2,1)S(1)}, bf16[4,1,64,512]{3,2,1,0:T(8,128)(2,1)S(1)}, u32[]{:S(2)}, u32[]{:S(2)}) %collective-permute-start.2) | collective-permute-done | bytes 262176 | tf_op jit(solution)/shard_map/ppermute | solution.py:28
  83.2 0.7 constant_dynamic-update-slice_fusion.26
  97.0 0.7 constant_dynamic-update-slice_fusion.6
  101.8 43.8 %all-gather.2.cloned.1.call-done = bf16[13824,256]{1,0:T(8,128)(2,1)} async-done(((bf16[3456,256]{1,0:T(8,128)(2,1)}), bf16[13824,256]{1,0:T(8,128)(2,1)}) %all-gather.2.cloned.1.call-update) | async-done | bytes 7077904 | tf_op jit(solution)/shard_map/all_gather | solution.py:137
  145.6 5.2 %convert_reduce_fusion = (f32[2,256]{1,0:T(2,128)S(1)}, bf16[2,1,64,256]{3,2,1,0:T(8,128)(2,1)S(1)}) fusion(bf16[2,1,64,256]{3,2,1,0:T(8,128)(2,1)S(1)} %copy-done.1, f32[256]{0:T(256)S(1)} %copy-done.5, bf16[13824,256]{1,0:T(8,128)(2,1)} %all-gather.2.cloned.1.call-done, bf16[128,13824]{1,0:T(8,128)(2,1)} %constant_dynamic-update-slice_fusion), kind=kOutput, calls=%fused_computation.49 | convolution fusion | flops 906165760 | bytes 10750976 | tf_op jit(solution)/shard_map/dot_general | solution.py:135
  151.0 8.7 %psum.38 = f32[2,16]{1,0:T(2,128)S(1)} all-reduce(f32[2,16]{1,0:T(2,128)S(1)} %reduce_sum.81), channel_id=1, replica_groups=mesh['clips'=2,'rows'=4,'tm'=2,'chan'=2] {'rows'}, use_global_device_ids=true, to_apply=%region_9.10 | all-reduce | flops 32 | bytes 256 | tf_op jit(solution)/shard_map/psum | solution.py:64
  160.1 10.0 %psum.39 = f32[2,16]{1,0:T(2,128)S(1)} all-reduce(f32[2,16]{1,0:T(2,128)S(1)} %reduce_sum.84), channel_id=1, replica_groups=mesh['clips'=2,'rows'=4,'tm'=2,'chan'=2] {'rows'}, use_global_device_ids=true, to_apply=%region_12.13 | all-reduce | flops 32 | bytes 256 | tf_op jit(solution)/shard_map/psum | solution.py:66
  170.4 3.8 %all_to_all.24 = bf16[2,1,64,256]{3,2,1,0:T(8,128)(2,1)S(1)} all-to-all(bf16[2,1,64,256]{3,2,1,0:T(8,128)(2,1)S(1)} %fusion.38), channel_id=1, replica_groups=mesh['clips'=2,'rows'=4,'tm'=2,'chan'=2] {'chan'}, dimensions={0} | all-to-all | bytes 131072 | tf_op jit(solution)/shard_map/all_to_all | solution.py:144
  174.3 14.3 %all_gather.11 = bf16[1,256,512]{2,1,0:T(8,128)(2,1)S(1)} all-gather(bf16[1,64,512]{2,1,0:T(8,128)(2,1)S(1)} %reshape.270), channel_id=1, replica_groups=mesh['clips'=2,'rows'=4,'tm'=2,'chan'=2] {'rows'}, dimensions={1}, use_global_device_ids=true | all-gather | bytes 327680 | tf_op jit(solution)/shard_map/all_gather | solution.py:160
  191.0 1.4 reduce.14
  192.6 3.8 %all_to_all.25 = bf16[2,2,8192]{2,1,0:T(2,128)(2,1)S(1)} all-to-all(bf16[2,2,8192]{2,1,0:T(2,128)(2,1)S(1)} %reshape.275), channel_id=1, replica_groups=mesh['clips'=2,'rows'=4,'tm'=2,'chan'=2] {'chan'}, dimensions={0} | all-to-all | bytes 131072 | tf_op jit(solution)/shard_map/all_to_all | solution.py:180
  (94 shorter events, 23.2 us)
Async XLA Ops:
  6.5 182.1 %copy-start = (bf16[512,512]{1,0:T(8,128)(2,1)S(1)}, bf16[512,512]{1,0:T(8,128)(2,1)}, u32[]{:S(2)}) copy-start(bf16[512,512]{1,0:T(8,128)(2,1)} %param.21) | copy-start | bytes 1572868
  6.5 139.1 %all-gather.2.cloned.1.call-start = ((), (), s32[]{:S(2)}) async-start(), calls=%async_computation.2 | async-start | bytes 8847360 | tf_op jit(solution)/shard_map/all_gather | solution.py:137
  49.9 6.5 %collective-permute-start = (bf16[2,1,64,512]{3,2,1,0:T(8,128)(2,1)S(1)}, bf16[2,1,64,512]{3,2,1,0:T(8,128)(2,1)S(1)}, u32[]{:S(2)}, u32[]{:S(2)}) collective-permute-start(bf16[2,1,64,512]{3,2,1,0:T(8,128)(2,1)S(1)} %all_gather.9), channel_id=1, source_target_pairs={{0,2},{1,3},{4,6},{5,7},{8,10},{9,11},{12,14},{13,15},{16,18},{17,... | collective-permute-start | bytes 393224 | tf_op jit(solution)/shard_map/ppermute | solution.py:15
  56.4 15.1 %collective-permute-start.1 = (bf16[4,1,64,512]{3,2,1,0:T(8,128)(2,1)S(1)}, bf16[4,1,64,512]{3,2,1,0:T(8,128)(2,1)S(1)}, u32[]{:S(2)}, u32[]{:S(2)}) collective-permute-start(bf16[4,1,64,512]{3,2,1,0:T(8,128)(2,1)S(1)} %pad_maximum_fusion.6), channel_id=1, source_target_pairs={{0,4},{4,8},{8,12},{1,5},{5,9},{9,13},{2,6},{6,10},{10,14},{3,7},{... | collective-permute-start | bytes 786440 | tf_op jit(solution)/shard_map/ppermute | solution.py:26
  59.8 22.5 %collective-permute-start.2 = (bf16[4,1,64,512]{3,2,1,0:T(8,128)(2,1)S(1)}, bf16[4,1,64,512]{3,2,1,0:T(8,128)(2,1)S(1)}, u32[]{:S(2)}, u32[]{:S(2)}) collective-permute-start(bf16[4,1,64,512]{3,2,1,0:T(8,128)(2,1)S(1)} %pad_maximum_fusion.6), channel_id=1, source_target_pairs={{4,0},{8,4},{12,8},{5,1},{9,5},{13,9},{6,2},{10,6},{14,10},{7,3},{... | collective-permute-start | bytes 786440 | tf_op jit(solution)/shard_map/ppermute | solution.py:28
  84.0 61.7 %copy-start.1 = (bf16[2,1,64,256]{3,2,1,0:T(8,128)(2,1)S(1)}, bf16[2,1,64,256]{3,2,1,0:T(8,128)(2,1)}, u32[]{:S(2)}) copy-start(bf16[2,1,64,256]{3,2,1,0:T(8,128)(2,1)} %param.14) | copy-start | bytes 196612
  84.0 61.6 %copy-start.5 = (f32[256]{0:T(256)S(1)}, f32[256]{0:T(256)}, u32[]{:S(2)}) copy-start(f32[256]{0:T(256)} %param.18) | copy-start | bytes 3076
  101.8 68.5 %copy-start.6 = (f32[256]{0:T(256)S(1)}, f32[256]{0:T(256)}, u32[]{:S(2)}) copy-start(f32[256]{0:T(256)} %param.20) | copy-start | bytes 3076
  101.8 68.5 %copy-start.7 = (f32[256]{0:T(256)S(1)}, f32[256]{0:T(256)}, u32[]{:S(2)}) copy-start(f32[256]{0:T(256)} %param.19) | copy-start | bytes 3076
  101.8 86.8 %copy-start.3 = (f32[512]{0:T(512)S(1)}, f32[512]{0:T(512)}, u32[]{:S(2)}) copy-start(f32[512]{0:T(512)} %param.22) | copy-start | bytes 6148
  101.8 87.1 %copy-start.8 = (bf16[512,512]{1,0:T(8,128)(2,1)S(1)}, bf16[512,512]{1,0:T(8,128)(2,1)}, u32[]{:S(2)}) copy-start(bf16[512,512]{1,0:T(8,128)(2,1)} %param.23) | copy-start | bytes 1572868
  101.8 87.8 %copy-start.9 = (bf16[512,512]{1,0:T(8,128)(2,1)S(1)}, bf16[512,512]{1,0:T(8,128)(2,1)}, u32[]{:S(2)}) copy-start(bf16[512,512]{1,0:T(8,128)(2,1)} %param.24) | copy-start | bytes 1572868
  101.8 87.8 %copy-start.10 = (f32[512]{0:T(512)S(1)}, f32[512]{0:T(512)}, u32[]{:S(2)}) copy-start(f32[512]{0:T(512)} %param.25) | copy-start | bytes 6148
  150.8 39.2 %copy-start.2 = (bf16[512,512]{1,0:T(8,128)(2,1)S(1)}, bf16[512,512]{1,0:T(8,128)(2,1)}, u32[]{:S(2)}) copy-start(bf16[512,512]{1,0:T(8,128)(2,1)} %param.26) | copy-start | bytes 1572868
  150.8 39.2 %copy-start.4 = (f32[512]{0:T(512)S(1)}, f32[512]{0:T(512)}, u32[]{:S(2)}) copy-start(f32[512]{0:T(512)} %param.27) | copy-start | bytes 6148
Sparse Core Ops, SparseCore 0:
  8.9 136.6 all-gather.1
